TPU v7x, 32 devices: a whole 2x2x4 slice. The times are simulated.
32 devices in a mesh: shard: 4 (over z), rep: 8 (over y, x, core).
Axes of the slice: x: 2, y: 2, z: 4, core: 2. Of those that a mesh axis runs over, the one named last changes fastest.
Arguments:
- grads: bfloat16 [1, 8192, 28672], P(None, 'shard', 'rep'), may hold values from -81 to 81
- seeds: int32 [1], replicated, may hold values from 0 to 999999
Outputs:
- projected: bfloat16 [512, 1, 28672], P('shard', None, 'rep')
All inputs are finite; a program needn't handle non-finite values.
Results may differ from a plain program's by a relative error of at most 0.0056.
Values may be sent and summed in bfloat16 or wider, within the bound.
No kernel may reach another device: no remote copies, remote signals or barrier semaphores. Data moves between devices by JAX's collectives and lax.ppermute only.
A program may use at most 128 MiB of HBM per device.

v0:
```python
import jax
import jax.numpy as jnp
from jax import lax
from jax.sharding import PartitionSpec as P

RANK = 512
mix_first = 668265263
mix_second = -2048144789
mix_third = -1028477387


def sketch_table(seeds, first_row, count, rank):
    rows = first_row + lax.iota(jnp.int32, count)
    columns = lax.iota(jnp.int32, rank)
    counter = rows[:, None] * jnp.int32(rank) + columns[None, :]
    hashed = jnp.bitwise_xor(counter[None, :, :], (seeds * jnp.int32(mix_first))[:, None, None])
    hashed = hashed * jnp.int32(mix_second)
    hashed = jnp.bitwise_xor(hashed, lax.shift_right_logical(hashed, jnp.int32(15)))
    hashed = hashed * jnp.int32(mix_third)
    hashed = jnp.bitwise_xor(hashed, lax.shift_right_logical(hashed, jnp.int32(13)))
    unit = lax.shift_right_logical(hashed, jnp.int32(8)).astype(jnp.float32) * (1.0 / 16777216.0)
    return (2.0 * unit - 1.0).astype(jnp.bfloat16)


def body(grads, seeds):
    mats, depth, width = grads.shape
    col0 = lax.axis_index("rep") * width
    outs = []
    for m in range(mats):
        table = sketch_table(seeds[m : m + 1], col0, width, RANK)[0]
        g = grads[m]
        partial = jnp.dot(g, table, preferred_element_type=jnp.float32)
        sketch_rows = lax.psum(partial, "rep")
        local_gram = jnp.dot(
            sketch_rows.T,
            sketch_rows,
            precision=lax.Precision.HIGHEST,
            preferred_element_type=jnp.float32,
        )
        piece = local_gram.shape[0] // lax.axis_size("rep")
        mine = lax.dynamic_slice_in_dim(local_gram, lax.axis_index("rep") * piece, piece, 0)
        gram = lax.all_gather(lax.psum(mine, "shard"), "rep", axis=0, tiled=True)
        factor = jnp.linalg.cholesky(gram)
        basis_rows = lax.linalg.triangular_solve(
            factor, sketch_rows, left_side=False, lower=True, transpose_a=True
        ).astype(jnp.bfloat16)
        partial_sum = jnp.dot(basis_rows.T, g, preferred_element_type=jnp.float32)
        outs.append(partial_sum)
    partial_sum = jnp.stack(outs, axis=1)
    projected = lax.psum_scatter(partial_sum, "shard", scatter_dimension=0, tiled=True)
    return projected.astype(jnp.bfloat16)


def solution(mesh):
    return jax.shard_map(
        body,
        mesh=mesh,
        in_specs=(P(None, "shard", "rep"), P()),
        out_specs=P("shard", None, "rep"),
        check_vma=False,
    )
```

profile of v0, /device:TPU:0, one launch (start us, length us, event | category | flops | bytes accessed | tf_op | source)
XLA Modules:
  0.0 482.1 jit_solution(17405715005233900256)
XLA Ops:
  6.5 0.0 all-reduce.4.cloned.1.call-start
  7.2 16.7 %fusion.24 = f32[2048,512]{0,1:T(8,128)} fusion(bf16[1,2048,3584]{2,1,0:T(8,128)(2,1)} %param.2, s32[]{:T(128)} %bitcast, s32[3584]{0:T(1024)S(1)} %add_multiply_fusion), kind=kOutput, calls=%fused_computation.25 | convolution fusion | flops 7540047872 | bytes 18888708 | tf_op jit(solution)/shard_map/dot_general | solution.py:32
  23.9 0.0 all-reduce.4.cloned.1.call-update
  23.9 0.3 all-reduce.6.cloned.1.call-start
  24.3 83.4 %all-reduce.4.cloned.1.call-done = f32[2048,512]{0,1:T(8,128)} async-done(((f32[2048,512]{0,1:T(8,128)}), f32[2048,512]{0,1:T(8,128)}) %all-reduce.4.cloned.1.call-update) | async-done | bytes 4194320 | tf_op jit(solution)/shard_map/psum | solution.py:33
  107.6 9.3 %fusion.81 = f32[512,512]{1,0:T(8,128)S(1)} fusion(f32[2048,512]{0,1:T(8,128)} %all-reduce.4.cloned.1.call-done), kind=kOutput, calls=%fused_computation.111 | convolution fusion | flops 6442450944 | bytes 5242880 | tf_op jit(solution)/shard_map/dot_general | solution.py:34
  117.0 0.7 constant_dynamic-slice_fusion.1
  117.7 0.0 all-reduce.6.cloned.1.call-update
  117.7 0.0 all-gather.2.cloned.1.call-start
  117.7 34.8 %all-reduce.6.cloned.1.call-done = f32[64,512]{1,0:T(8,128)} async-done(((f32[64,512]{1,0:T(8,128)}), f32[64,512]{1,0:T(8,128)}) %all-reduce.6.cloned.1.call-update) | async-done | bytes 131088 | tf_op jit(solution)/shard_map/psum | solution.py:42
  152.6 0.0 all-gather.2.cloned.1.call-update
  152.6 0.0 reduce-scatter.2.cloned.1.call-start
  152.6 24.9 %all-gather.2.cloned.1.call-done = f32[512,512]{1,0:T(8,128)} async-done(((f32[64,512]{1,0:T(8,128)}), f32[512,512]{1,0:T(8,128)}) %all-gather.2.cloned.1.call-update) | async-done | bytes 1048592 | tf_op jit(solution)/shard_map/all_gather | solution.py:42
  177.5 1.6 copy.7
  179.1 1.4 fusion.50
  180.6 11.7 %cholesky.104 = f32[128,128]{1,0:T(8,128)S(1)} custom-call(f32[128,128]{1,0:T(8,128)S(1)} %cholesky.266), custom_call_target="Cholesky" | custom-call | tf_op jit(solution)/shard_map/jit(cholesky)/cholesky | solution.py:43
  192.3 9.8 %custom-call.30 = f32[1,128,128]{1,2,0:T(8,128)S(1)} custom-call(f32[1,128,128]{2,1,0:T(8,128)S(1)} %get-tuple-element.32), custom_call_target="InvertDiagBlocksLowerTriangular" | custom-call | tf_op jit(solution)/shard_map/jit(cholesky)/cholesky | solution.py:43
  202.1 0.1 cholesky.224
  202.3 0.3 constant_dynamic-update-slice_fusion.3
  202.6 0.3 convolution_subtract_fusion.2
  202.9 11.7 %cholesky.217 = f32[128,128]{1,0:T(8,128)S(1)} custom-call(f32[128,128]{1,0:T(8,128)S(1)} %cholesky.270), custom_call_target="Cholesky" | custom-call | tf_op jit(solution)/shard_map/jit(cholesky)/cholesky | solution.py:43
  214.7 18.5 %custom-call.31 = f32[1,128,128]{1,2,0:T(8,128)S(1)} custom-call(f32[1,128,128]{2,1,0:T(8,128)S(1)} %get-tuple-element.29), custom_call_target="InvertDiagBlocksLowerTriangular" | custom-call | tf_op jit(solution)/shard_map/jit(cholesky)/cholesky | solution.py:43
  233.2 0.3 convolution_dynamic-update-slice_fusion
  233.5 0.4 convolution_subtract_fusion.3
  233.9 11.7 %cholesky.238 = f32[128,128]{1,0:T(8,128)S(1)} custom-call(f32[128,128]{1,0:T(8,128)S(1)} %cholesky.275), custom_call_target="Cholesky" | custom-call | tf_op jit(solution)/shard_map/jit(cholesky)/cholesky | solution.py:43
  245.6 0.7 compare_reduce_fusion.1
  246.3 9.8 %custom-call.32 = f32[1,128,128]{1,2,0:T(8,128)S(1)} custom-call(f32[1,128,128]{2,1,0:T(8,128)S(1)} %get-tuple-element.26), custom_call_target="InvertDiagBlocksLowerTriangular" | custom-call | tf_op jit(solution)/shard_map/jit(cholesky)/cholesky | solution.py:43
  256.1 0.2 convolution_dynamic-update-slice_fusion.1
  256.3 0.4 convolution_subtract_fusion.4
  256.7 11.7 %cholesky.255 = f32[128,128]{1,0:T(8,128)S(1)} custom-call(f32[128,128]{1,0:T(8,128)S(1)} %convolution_subtract_fusion.4), custom_call_target="Cholesky" | custom-call | tf_op jit(solution)/shard_map/jit(cholesky)/cholesky | solution.py:43
  268.4 0.7 compare_reduce_fusion
  269.1 0.7 compare_reduce_fusion.2
  272.4 0.3 select_select_fusion
  272.7 7.9 %while.1 = (s32[]{:T(128)}, f32[512,512]{1,0:T(8,128)S(1)}, s32[4,2]{0,1:T(2,128)S(1)}, f32[4,128,128]{2,1,0:T(8,128)S(1)}, s32[]{:T(128)}) while((s32[]{:T(128)}, f32[512,512]{1,0:T(8,128)S(1)}, s32[4,2]{0,1:T(2,128)S(1)}, f32[4,128,128]{2,1,0:T(8,128)S(1)}, s32[]{:T(128)}) %tuple.30), condition=%wide.while_cond, body=%wide.while_body.sunk | while | flops 2 | bytes 131189 | solution.py:44
  272.8 0.1 constant_dynamic-slice_fusion.3
  272.8 0.5 fusion.90
  273.4 1.4 bitcast_dynamic-update-slice_fusion.2
  274.7 0.1 constant_dynamic-slice_fusion.3
  274.8 0.5 fusion.90
  275.3 1.4 bitcast_dynamic-update-slice_fusion.2
  276.7 0.1 constant_dynamic-slice_fusion.3
  276.8 0.5 fusion.90
  277.3 1.4 bitcast_dynamic-update-slice_fusion.2
  278.7 0.1 constant_dynamic-slice_fusion.3
  278.8 0.5 fusion.90
  279.3 1.4 bitcast_dynamic-update-slice_fusion.2
  280.7 39.3 %custom-call.33 = f32[4,128,128]{1,2,0:T(8,128)S(1)} custom-call(f32[4,128,128]{2,1,0:T(8,128)S(1)} %get-tuple-element.12), custom_call_target="InvertDiagBlocksLowerTriangular" | custom-call | tf_op jit(solution)/shard_map/triangular_solve | solution.py:44
  320.0 0.0 copy-start
  320.0 2.5 fusion.80
  322.4 2.3 convolution_subtract_fusion.1
  324.8 1.1 fusion.79
  325.8 0.0 copy-done
  325.8 1.3 convolution_subtract_fusion
  327.2 1.1 fusion.78
  328.3 2.2 fusion.35
  330.5 1.1 convolution_convert_fusion
  331.6 13.1 %fusion.10 = f32[512,1,3584]{2,0,1:T(8,128)} fusion(bf16[1,2048,3584]{2,1,0:T(8,128)(2,1)} %param.2, bf16[2048,128]{0,1:T(8,128)(2,1)S(1)} %convolution_convert_fusion, bf16[2048,128]{0,1:T(8,128)(2,1)S(1)} %get-tuple-element.35, bf16[2048,128]{0,1:T(8,128)(2,1)S(1)} %get-tuple-element.37, bf16[2048,128]{0,1:T(8,128)(2,1)S(1)} %get-tuple-element.39), kind=kOutput, calls=%fused_computation.14 | convolution fusion | flops 7524581376 | bytes 24117248 | tf_op jit(solution)/shard_map/dot_general | solution.py:47
  344.7 0.0 reduce-scatter.2.cloned.1.call-update
  344.7 127.9 %reduce-scatter.2.cloned.1.call-done = f32[128,1,3584]{2,0,1:T(8,128)} async-done(((f32[512,1,3584]{2,0,1:T(8,128)}), f32[128,1,3584]{2,0,1:T(8,128)}) %reduce-scatter.2.cloned.1.call-update) | async-done | bytes 1835024 | tf_op jit(solution)/shard_map/reduce_scatter | solution.py:50
  472.6 2.5 convert_element_type.47
  (11 shorter events, 0.2 us)
Async XLA Ops:
  6.5 101.1 %all-reduce.4.cloned.1.call-start = ((), (), s32[]{:S(2)}) async-start(), calls=%async_computation.1 | async-start | bytes 8388608 | tf_op jit(solution)/shard_map/psum | solution.py:33
  23.9 128.6 %all-reduce.6.cloned.1.call-start = ((), (), s32[]{:S(2)}) async-start(), calls=%async_computation.2 | async-start | bytes 262144 | tf_op jit(solution)/shard_map/psum | solution.py:42
  117.7 59.9 %all-gather.2.cloned.1.call-start = ((), (), s32[]{:S(2)}) async-start(), calls=%async_computation.3 | async-start | bytes 1179648 | tf_op jit(solution)/shard_map/all_gather | solution.py:42
  152.6 320.0 %reduce-scatter.2.cloned.1.call-start = ((), (), s32[]{:S(2)}) async-start(), calls=%async_computation.4 | async-start | bytes 9175040 | tf_op jit(solution)/shard_map/reduce_scatter | solution.py:50
  320.0 5.9 %copy-start = (f32[2048,512]{0,1:T(8,128)S(1)}, f32[2048,512]{0,1:T(8,128)}, u32[]{:S(2)}) copy-start(f32[2048,512]{0,1:T(8,128)} %all-reduce.4.cloned.1.call-done) | copy-start | bytes 12582916
Sparse Core Ops, SparseCore 0:
  24.1 83.5 all-reduce.3
  117.8 34.7 all-reduce.5
  154.5 23.0 all-gather.1
  344.8 127.7 reduce-scatter.1
where the time goes:
time: 490 us; the launch traced here: 482 us
  waiting for transfers between devices  271 us (55%)
  other arithmetic  131 us (27%)
  matrix products  52.5 us (11%)
  between operations  17 us (3%)
  local copies, waits for them, and re-layouts  10.2 us (2%)
    reduce_scatter x1, waiting for transfers between devices, body(): lax.psum_scatter(partial_sum, 'shard', scatter_dimension=0, tiled=True)  128 us
    another operation x14, other arithmetic, body(): factor = jnp.linalg.cholesky(gram)  87.2 us
    psum x1, waiting for transfers between devices, body(): sketch_rows = lax.psum(partial, 'rep')  83.4 us
    another operation x3, other arithmetic, body(): lax.linalg.triangular_solve(factor, sketch_rows, left_side=False, lower=T...  39.7 us
    psum x1, waiting for transfers between devices, body(): gram = lax.all_gather(lax.psum(mine, 'shard'), 'rep', axis=0, tiled=True)  34.8 us
    all_gather x1, waiting for transfers between devices, body(): gram = lax.all_gather(lax.psum(mine, 'shard'), 'rep', axis=0, tiled=True)  24.9 us
    dot_general x1, matrix products, body(): partial = jnp.dot(g, table, preferred_element_type=jnp.float32)  16.7 us
    dot_general x1, matrix products, body(): partial_sum = jnp.dot(basis_rows.T, g, preferred_element_type=jnp.float32)  13.1 us
  transfers between devices with their start and end apart: 4, of which 4 were waited for; matrix products, arithmetic and copies ran while one was open for 0% of the time, Pallas kernels for 0%

commit v1 on v0

--- a/solution.py
+++ b/solution.py
@@ -39,7 +39,9 @@
         )
         piece = local_gram.shape[0] // lax.axis_size("rep")
         mine = lax.dynamic_slice_in_dim(local_gram, lax.axis_index("rep") * piece, piece, 0)
-        gram = lax.all_gather(lax.psum(mine, "shard"), "rep", axis=0, tiled=True)
+        gram = lax.all_gather(
+            jnp.sum(lax.all_gather(mine, "shard"), axis=0), "rep", axis=0, tiled=True
+        )
         factor = jnp.linalg.cholesky(gram)
         basis_rows = lax.linalg.triangular_solve(
             factor, sketch_rows, left_side=False, lower=True, transpose_a=True

time: 490 us -> 470 us (0.959)
  waiting for transfers between devices: 271 us -> 236 us
  blocking collectives: 0 us -> 15.5 us
    psum x1 -> x0, waiting for transfers between devices: 34.8 us -> none  [body(): gram = lax.all_gather(lax.psum(mine, 'shard'), 'rep', axis=0, tiled=True)]
    all_gather x0 -> x1, blocking collectives: none -> 15.5 us  [body(): lax.all_gather(mine, 'shard')]
  transfers between devices with their start and end apart: 4 -> 3, of which waited for: 4 -> 3; matrix products, arithmetic and copies ran while one was open for 0% -> 0% of each run, Pallas kernels for 0% -> 0%
where the time goes in v1:
time: 470 us; the launch traced here: 462 us
  waiting for transfers between devices  236 us (50%)
  other arithmetic  131 us (28%)
  matrix products  52.5 us (11%)
  between operations  17 us (4%)
  blocking collectives  15.5 us (3%)
  local copies, waits for them, and re-layouts  9.54 us (2%)
    reduce_scatter x1, waiting for transfers between devices, body(): lax.psum_scatter(partial_sum, 'shard', scatter_dimension=0, tiled=True)  128 us
    another operation x14, other arithmetic, body(): factor = jnp.linalg.cholesky(gram)  87.2 us
    psum x1, waiting for transfers between devices, body(): sketch_rows = lax.psum(partial, 'rep')  83.4 us
    another operation x3, other arithmetic, body(): lax.linalg.triangular_solve(factor, sketch_rows, left_side=False, lower=T...  39.7 us
    all_gather x1, waiting for transfers between devices, body(): lax.all_gather(jnp.sum(lax.all_gather(mine, 'shard'), axis=0), 'rep', axi...  24.3 us
    dot_general x1, matrix products, body(): partial = jnp.dot(g, table, preferred_element_type=jnp.float32)  16.7 us
    all_gather x1, blocking collectives, body(): lax.all_gather(mine, 'shard')  15.5 us
    dot_general x1, matrix products, body(): partial_sum = jnp.dot(basis_rows.T, g, preferred_element_type=jnp.float32)  13.1 us
  transfers between devices with their start and end apart: 3, of which 3 were waited for; matrix products, arithmetic and copies ran while one was open for 0% of the time, Pallas kernels for 0%

profile of v1, /device:TPU:0, one launch (start us, length us, event | category | flops | bytes accessed | tf_op | source)
XLA Modules:
  0.0 462.1 jit_solution(8474444974185486328)
XLA Ops:
  6.5 0.0 all-reduce.3.cloned.1.call-start
  7.2 16.7 %fusion.24 = f32[2048,512]{0,1:T(8,128)} fusion(bf16[1,2048,3584]{2,1,0:T(8,128)(2,1)} %param.2, s32[]{:T(128)} %bitcast, s32[3584]{0:T(1024)S(1)} %add_multiply_fusion), kind=kOutput, calls=%fused_computation.25 | convolution fusion | flops 7540047872 | bytes 18888708 | tf_op jit(solution)/shard_map/dot_general | solution.py:32
  23.9 0.0 all-reduce.3.cloned.1.call-update
  23.9 0.3 all-gather.3.cloned.1.call-start
  24.3 83.4 %all-reduce.3.cloned.1.call-done = f32[2048,512]{0,1:T(8,128)} async-done(((f32[2048,512]{0,1:T(8,128)}), f32[2048,512]{0,1:T(8,128)}) %all-reduce.3.cloned.1.call-update) | async-done | bytes 4194320 | tf_op jit(solution)/shard_map/psum | solution.py:33
  107.6 9.3 %fusion.81 = f32[512,512]{1,0:T(8,128)S(1)} fusion(f32[2048,512]{0,1:T(8,128)} %all-reduce.3.cloned.1.call-done), kind=kOutput, calls=%fused_computation.111 | convolution fusion | flops 6442450944 | bytes 5242880 | tf_op jit(solution)/shard_map/dot_general | solution.py:34
  117.0 15.5 %all-gather = f32[256,512]{1,0:T(8,128)S(1)} all-gather(f32[64,512]{1,0:T(8,128)S(1)} %constant_dynamic-slice_fusion.1), channel_id=2, replica_groups=mesh['shard'=4,'rep'=8] {'shard'}, dimensions={0}, use_global_device_ids=true | all-gather | bytes 655360 | tf_op jit(solution)/shard_map/all_gather | solution.py:43
  132.5 0.7 reduce_sum.9
  133.2 0.0 all-gather.3.cloned.1.call-update
  133.2 0.0 reduce-scatter.2.cloned.1.call-start
  133.3 24.3 %all-gather.3.cloned.1.call-done = f32[512,512]{1,0:T(8,128)} async-done(((f32[64,512]{1,0:T(8,128)}), f32[512,512]{1,0:T(8,128)}) %all-gather.3.cloned.1.call-update) | async-done | bytes 1048592 | tf_op jit(solution)/shard_map/all_gather | solution.py:42
  157.6 1.6 copy.5
  159.1 1.4 fusion.50
  160.6 11.7 %cholesky.104 = f32[128,128]{1,0:T(8,128)S(1)} custom-call(f32[128,128]{1,0:T(8,128)S(1)} %cholesky.266), custom_call_target="Cholesky" | custom-call | tf_op jit(solution)/shard_map/jit(cholesky)/cholesky | solution.py:45
  172.3 0.1 cholesky.224
  172.5 9.8 %custom-call.30 = f32[1,128,128]{1,2,0:T(8,128)S(1)} custom-call(f32[1,128,128]{2,1,0:T(8,128)S(1)} %get-tuple-element.32), custom_call_target="InvertDiagBlocksLowerTriangular" | custom-call | tf_op jit(solution)/shard_map/jit(cholesky)/cholesky | solution.py:45
  182.3 0.3 constant_dynamic-update-slice_fusion.3
  182.6 0.3 convolution_subtract_fusion.2
  182.9 11.7 %cholesky.217 = f32[128,128]{1,0:T(8,128)S(1)} custom-call(f32[128,128]{1,0:T(8,128)S(1)} %cholesky.270), custom_call_target="Cholesky" | custom-call | tf_op jit(solution)/shard_map/jit(cholesky)/cholesky | solution.py:45
  194.7 18.5 %custom-call.31 = f32[1,128,128]{1,2,0:T(8,128)S(1)} custom-call(f32[1,128,128]{2,1,0:T(8,128)S(1)} %get-tuple-element.29), custom_call_target="InvertDiagBlocksLowerTriangular" | custom-call | tf_op jit(solution)/shard_map/jit(cholesky)/cholesky | solution.py:45
  213.2 0.3 convolution_dynamic-update-slice_fusion
  213.5 0.4 convolution_subtract_fusion.3
  213.9 11.7 %cholesky.238 = f32[128,128]{1,0:T(8,128)S(1)} custom-call(f32[128,128]{1,0:T(8,128)S(1)} %cholesky.275), custom_call_target="Cholesky" | custom-call | tf_op jit(solution)/shard_map/jit(cholesky)/cholesky | solution.py:45
  225.6 0.7 compare_reduce_fusion.1
  226.3 9.8 %custom-call.32 = f32[1,128,128]{1,2,0:T(8,128)S(1)} custom-call(f32[1,128,128]{2,1,0:T(8,128)S(1)} %get-tuple-element.26), custom_call_target="InvertDiagBlocksLowerTriangular" | custom-call | tf_op jit(solution)/shard_map/jit(cholesky)/cholesky | solution.py:45
  236.1 0.2 convolution_dynamic-update-slice_fusion.1
  236.3 0.4 convolution_subtract_fusion.4
  236.7 11.7 %cholesky.255 = f32[128,128]{1,0:T(8,128)S(1)} custom-call(f32[128,128]{1,0:T(8,128)S(1)} %convolution_subtract_fusion.4), custom_call_target="Cholesky" | custom-call | tf_op jit(solution)/shard_map/jit(cholesky)/cholesky | solution.py:45
  248.4 0.7 compare_reduce_fusion
  249.1 0.7 compare_reduce_fusion.2
  252.4 0.3 select_select_fusion
  252.8 7.9 %while.1 = (s32[]{:T(128)}, f32[512,512]{1,0:T(8,128)S(1)}, s32[4,2]{0,1:T(2,128)S(1)}, f32[4,128,128]{2,1,0:T(8,128)S(1)}, s32[]{:T(128)}) while((s32[]{:T(128)}, f32[512,512]{1,0:T(8,128)S(1)}, s32[4,2]{0,1:T(2,128)S(1)}, f32[4,128,128]{2,1,0:T(8,128)S(1)}, s32[]{:T(128)}) %tuple.30), condition=%wide.while_cond, body=%wide.while_body.sunk | while | flops 2 | bytes 131189 | solution.py:46
  252.8 0.1 constant_dynamic-slice_fusion.3
  252.8 0.5 fusion.90
  253.4 1.4 bitcast_dynamic-update-slice_fusion.2
  254.7 0.1 constant_dynamic-slice_fusion.3
  254.8 0.5 fusion.90
  255.3 1.4 bitcast_dynamic-update-slice_fusion.2
  256.7 0.1 constant_dynamic-slice_fusion.3
  256.8 0.5 fusion.90
  257.3 1.4 bitcast_dynamic-update-slice_fusion.2
  258.7 0.1 constant_dynamic-slice_fusion.3
  258.8 0.5 fusion.90
  259.3 1.4 bitcast_dynamic-update-slice_fusion.2
  260.7 39.3 %custom-call.33 = f32[4,128,128]{1,2,0:T(8,128)S(1)} custom-call(f32[4,128,128]{2,1,0:T(8,128)S(1)} %get-tuple-element.12), custom_call_target="InvertDiagBlocksLowerTriangular" | custom-call | tf_op jit(solution)/shard_map/triangular_solve | solution.py:46
  300.0 0.0 copy-start
  300.0 2.5 fusion.80
  302.5 2.3 convolution_subtract_fusion.1
  304.8 1.1 fusion.79
  305.8 0.0 copy-done
  305.9 1.3 convolution_subtract_fusion
  307.2 1.1 fusion.78
  308.3 2.2 fusion.35
  310.5 1.1 convolution_convert_fusion
  311.6 13.1 %fusion.10 = f32[512,1,3584]{2,0,1:T(8,128)} fusion(bf16[1,2048,3584]{2,1,0:T(8,128)(2,1)} %param.2, bf16[2048,128]{0,1:T(8,128)(2,1)S(1)} %convolution_convert_fusion, bf16[2048,128]{0,1:T(8,128)(2,1)S(1)} %get-tuple-element.35, bf16[2048,128]{0,1:T(8,128)(2,1)S(1)} %get-tuple-element.37, bf16[2048,128]{0,1:T(8,128)(2,1)S(1)} %get-tuple-element.39), kind=kOutput, calls=%fused_computation.14 | convolution fusion | flops 7524581376 | bytes 24117248 | tf_op jit(solution)/shard_map/dot_general | solution.py:49
  324.7 0.0 reduce-scatter.2.cloned.1.call-update
  324.7 127.9 %reduce-scatter.2.cloned.1.call-done = f32[128,1,3584]{2,0,1:T(8,128)} async-done(((f32[512,1,3584]{2,0,1:T(8,128)}), f32[128,1,3584]{2,0,1:T(8,128)}) %reduce-scatter.2.cloned.1.call-update) | async-done | bytes 1835024 | tf_op jit(solution)/shard_map/reduce_scatter | solution.py:52
  452.6 2.5 convert_element_type.47
  (12 shorter events, 0.2 us)
Async XLA Ops:
  6.5 101.1 %all-reduce.3.cloned.1.call-start = ((), (), s32[]{:S(2)}) async-start(), calls=%async_computation.1 | async-start | bytes 8388608 | tf_op jit(solution)/shard_map/psum | solution.py:33
  23.9 133.6 %all-gather.3.cloned.1.call-start = ((), (), s32[]{:S(2)}) async-start(), calls=%async_computation.2 | async-start | bytes 1179648 | tf_op jit(solution)/shard_map/all_gather | solution.py:42
  133.2 319.4 %reduce-scatter.2.cloned.1.call-start = ((), (), s32[]{:S(2)}) async-start(), calls=%async_computation.3 | async-start | bytes 9175040 | tf_op jit(solution)/shard_map/reduce_scatter | solution.py:52
  300.0 5.9 %copy-start = (f32[2048,512]{0,1:T(8,128)S(1)}, f32[2048,512]{0,1:T(8,128)}, u32[]{:S(2)}) copy-start(f32[2048,512]{0,1:T(8,128)} %all-reduce.3.cloned.1.call-done) | copy-start | bytes 12582916
Sparse Core Ops, SparseCore 0:
  24.1 83.5 all-reduce.2
  133.3 24.2 all-gather.2
  324.8 127.7 reduce-scatter.1
